TPU v7x, 256 devices: a whole 4x4x8 slice. The times are simulated.
256 devices in a mesh: sec: 2 (over y_lo), dp: 8 (over x, y_hi), seq: 16 (over z, core).
Axes of the slice: x: 4, y: 4 (y_hi: 2, y_lo: 2; y = y_hi * 2 + y_lo), z: 8, core: 2. Of those that a mesh axis runs over, the one named last changes fastest.
Arguments:
- hidden: bfloat16 [256, 128, 2560], P(('sec', 'dp', 'seq')), may hold values from -24 to 24
- cond_shift: bfloat16 [256, 2560], P(('sec', 'dp', 'seq')), may hold values from -0.3125 to 0.3125
- cond_scale: bfloat16 [256, 2560], P(('sec', 'dp', 'seq')), may hold values from -1.75 to 1.75
- noisy: bfloat16 [256, 128, 256], P(('sec', 'dp', 'seq')), may hold values from -6 to 6
- noise_level: float32 [256], P(('sec', 'dp', 'seq')), may hold values from 0.2 to 1
- w_out: bfloat16 [2560, 256], replicated, may hold values from -0.125 to 0.125
- w_embed: bfloat16 [256, 2048], replicated, may hold values from -0.375 to 0.375
- w_root: bfloat16 [2, 2048], replicated, may hold values from -0.03125 to 0.03125
- w_qkv: bfloat16 [3, 2048, 2048], P(None, None, 'seq'), may hold values from -0.125 to 0.125
- w_proj: bfloat16 [2048, 512], P('seq'), may hold values from -0.125 to 0.125
- text_table: bfloat16 [49408, 512], P('seq'), may hold values from -6 to 6
- text_ids: int32 [32, 32], replicated, may hold values from 0 to 49407
- prompt_index: int32 [256], P(('sec', 'dp')), may hold values from 0 to 31
- reward_weight: float32 [256], P(('sec', 'dp')), may hold values from 1000 to 4000
Outputs:
- rewards: float32 [256], P(('sec', 'dp'))
- grad_w_out: float32 [2560, 256], P('seq')
- grad_hidden: bfloat16 [256, 128, 2560], P(('sec', 'dp', 'seq'))
All inputs are finite; a program needn't handle non-finite values.
Results may differ from a plain program's by a relative error of at most 0.017.
The roundings to bfloat16 on the way count: a program that leaves them out, or rounds other values in their place, can miss the bound.
Values may be sent and summed in bfloat16 or wider, within the bound.
No kernel may reach another device: no remote copies, remote signals or barrier semaphores. Data moves between devices by JAX's collectives and lax.ppermute only.
A program may use at most 128 MiB of HBM per device.

v0:
```python
import jax
import jax.numpy as jnp
from jax import lax
from jax.sharding import PartitionSpec as P

D_REW = 2048
HEADS = 16
PROMPTS = 32
normalizing_sharpness = 10.0
epsilon = 1e-06
highest = lax.Precision.HIGHEST


def rotate(angle, first, second):
    cosine = jnp.cos(angle)
    sine_term = jnp.sin(angle)
    return (cosine * first + sine_term * second, cosine * second - sine_term * first)


def suffix(values):
    return jnp.sum(values, axis=1, keepdims=True) - jnp.cumsum(values, axis=1)


def local_path(motion):
    spin = motion[..., 0]
    theta = jnp.cumsum(spin, axis=1) - spin
    step_east, step_north = rotate(theta, motion[..., 1], motion[..., 2])
    path_east = jnp.cumsum(step_east, axis=1) - step_east
    path_north = jnp.cumsum(step_north, axis=1) - step_north
    return (theta, path_east, path_north)


def embed(motion, root_east, root_north, w_embed, root_rows):
    emb = jnp.einsum(
        "cfe,ed->cfd", motion.astype(jnp.bfloat16), w_embed, preferred_element_type=jnp.float32
    )
    emb = emb + root_east[..., None] * root_rows[0] + root_north[..., None] * root_rows[1]
    scale_rms = jnp.sqrt(jnp.mean(emb * emb, axis=-1, keepdims=True) + epsilon)
    return (emb / scale_rms, scale_rms)


def unit_rows(vectors):
    length = jnp.sqrt(jnp.sum(vectors * vectors, axis=-1, keepdims=True) + epsilon)
    return (vectors / length, length)


def norm_grad(grad, normed, scale_rms):
    return (grad - normed * jnp.mean(grad * normed, axis=-1, keepdims=True)) / scale_rms


def motion_grad(d_emb, normed_e, scale_rms, motion, theta, embed_rows, root_rows):
    d_unemb = norm_grad(d_emb, normed_e, scale_rms)
    d_embedded = jnp.einsum("cfd,ed->cfe", d_unemb, embed_rows, precision=highest)
    grad_east = suffix(jnp.sum(d_unemb * root_rows[0], axis=-1))
    grad_north = suffix(jnp.sum(d_unemb * root_rows[1], axis=-1))
    vel_east = motion[..., 1]
    vel_north = motion[..., 2]
    d_east, d_north = rotate(-theta, grad_east, grad_north)
    cosine = jnp.cos(theta)
    sine_term = jnp.sin(theta)
    d_theta = grad_east * (cosine * vel_north - sine_term * vel_east) - grad_north * (
        cosine * vel_east + sine_term * vel_north
    )
    d_spin = suffix(d_theta)
    return d_embedded.at[..., 0].add(d_spin).at[..., 1].add(d_east).at[..., 2].add(d_north)


def local(
    hidden,
    cond_shift,
    cond_scale,
    noisy,
    noise_level,
    w_out,
    w_embed,
    w_root,
    w_qkv,
    w_proj,
    text_table,
    text_ids,
    prompt_index,
    reward_weight,
):
    clips_dev = hidden.shape[0]
    ways = lax.axis_size("seq")
    group = clips_dev * ways
    frames = hidden.shape[1]
    width_cols = w_qkv.shape[2]
    head_size = D_REW // HEADS
    heads_dev = width_cols // head_size
    root_rows = w_root.astype(jnp.float32)
    embed_rows = w_embed.astype(jnp.float32)
    vocab_rows = text_table.shape[0]
    local_ids = text_ids - lax.axis_index("seq") * vocab_rows
    inside = (local_ids >= 0) & (local_ids < vocab_rows)
    picked = jnp.take(text_table, jnp.clip(local_ids, 0, vocab_rows - 1), axis=0).astype(
        jnp.float32
    )
    text_part = jnp.sum(jnp.where(inside[..., None], picked, 0.0), axis=1)
    text_raw = lax.psum(text_part, "seq")
    text_unit, text_len = unit_rows(text_raw)
    hidden_f = hidden.astype(jnp.float32)
    centred = hidden_f - jnp.mean(hidden_f, axis=-1, keepdims=True)
    inv_std = lax.rsqrt(jnp.mean(centred * centred, axis=-1, keepdims=True) + epsilon)
    normed_h = centred * inv_std
    gain = 1.0 + cond_scale.astype(jnp.float32)[:, None, :]
    modulated = (normed_h * gain + cond_shift.astype(jnp.float32)[:, None, :]).astype(jnp.bfloat16)
    eps_pred = jnp.einsum("cfd,de->cfe", modulated, w_out, preferred_element_type=jnp.float32)
    level = noise_level[:, None, None]
    x_clean = noisy.astype(jnp.float32) - level * eps_pred
    theta, path_east, path_north = local_path(x_clean)
    normed_e, scale_rms = embed(x_clean, path_east, path_north, w_embed, root_rows)
    projected = jnp.einsum(
        "cfd,jdk->cfjk",
        lax.all_gather(normed_e.astype(jnp.bfloat16), "seq", axis=0, tiled=True),
        w_qkv,
        preferred_element_type=jnp.float32,
    )
    projected = projected.reshape(group, frames, 3, heads_dev, head_size)
    query_unit, query_len = unit_rows(projected[:, :, 0])
    key_unit, key_len = unit_rows(projected[:, :, 1])
    asking_vectors_group = query_unit.astype(jnp.bfloat16)
    lookup_vectors_group = key_unit.astype(jnp.bfloat16)
    value_b = projected[:, :, 2].astype(jnp.bfloat16)
    similarity_table = normalizing_sharpness * jnp.einsum(
        "cfhd,cghd->chfg",
        asking_vectors_group,
        lookup_vectors_group,
        preferred_element_type=jnp.float32,
    )
    expo = jnp.exp(similarity_table)
    focus_probabilities = expo / jnp.sum(expo, axis=-1, keepdims=True)
    attention_b = focus_probabilities.astype(jnp.bfloat16)
    column_mass = jnp.sum(attention_b, axis=2, dtype=jnp.float32)
    value_f = value_b.astype(jnp.float32)
    pooled = jnp.einsum("chg,cghd->chd", column_mass, value_f, precision=highest)
    pooled_b = pooled.astype(jnp.bfloat16).reshape(group, width_cols)
    motion_part = jnp.dot(pooled_b, w_proj, preferred_element_type=jnp.float32)
    motion_emb = lax.psum(motion_part, "seq")
    choose = (prompt_index[:, None] == jnp.arange(PROMPTS)[None, :]).astype(jnp.float32)
    target = jnp.dot(choose, text_unit, precision=highest)
    emb_len = jnp.sqrt(jnp.sum(motion_emb * motion_emb, axis=-1) + epsilon)
    rewards = jnp.sum(motion_emb * target, axis=-1) / emb_len
    d_memb = (
        (-reward_weight)[:, None]
        * (target - rewards[:, None] * motion_emb / emb_len[:, None])
        / emb_len[:, None]
    )
    d_pooled = jnp.dot(d_memb, w_proj.astype(jnp.float32).T, precision=highest).reshape(
        group, heads_dev, head_size
    )
    reduction_dimension = jnp.einsum("chd,cghd->chg", d_pooled, value_f, precision=highest)
    d_value = jnp.transpose(column_mass, (0, 2, 1))[..., None] * d_pooled[:, None]
    pairwise_dot_similarity = jnp.sum(
        focus_probabilities * reduction_dimension[:, :, None, :], axis=-1, keepdims=True
    )
    similarity_derivative = (
        normalizing_sharpness
        * focus_probabilities
        * (reduction_dimension[:, :, None, :] - pairwise_dot_similarity)
    ).astype(jnp.bfloat16)
    d_qu = jnp.einsum(
        "chfg,cghd->cfhd",
        similarity_derivative,
        lookup_vectors_group,
        preferred_element_type=jnp.float32,
    )
    d_ku = jnp.einsum(
        "chfg,cfhd->cghd",
        similarity_derivative,
        asking_vectors_group,
        preferred_element_type=jnp.float32,
    )
    d_query = (d_qu - query_unit * jnp.sum(query_unit * d_qu, axis=-1, keepdims=True)) / query_len
    d_key = (d_ku - key_unit * jnp.sum(key_unit * d_ku, axis=-1, keepdims=True)) / key_len
    d_proj = (
        jnp.stack([d_query, d_key, d_value], axis=2)
        .astype(jnp.bfloat16)
        .reshape(group, frames, 3, width_cols)
    )
    d_emb = lax.psum_scatter(
        jnp.einsum("cfjk,jdk->cfd", d_proj, w_qkv, preferred_element_type=jnp.float32),
        "seq",
        scatter_dimension=0,
        tiled=True,
    )
    d_motion = motion_grad(d_emb, normed_e, scale_rms, x_clean, theta, embed_rows, root_rows)
    d_eps_b = (-level * d_motion).astype(jnp.bfloat16)
    d_mod = jnp.einsum("cfe,de->cfd", d_eps_b, w_out, preferred_element_type=jnp.float32)
    d_norm = d_mod * gain
    grad_hidden = (
        inv_std
        * (
            d_norm
            - jnp.mean(d_norm, axis=-1, keepdims=True)
            - normed_h * jnp.mean(d_norm * normed_h, axis=-1, keepdims=True)
        )
    ).astype(jnp.bfloat16)
    rows_dev = w_out.shape[0] // ways
    grad_term = jnp.einsum("cfd,cfe->de", modulated, d_eps_b, preferred_element_type=jnp.float32)
    grad_total = lax.psum(grad_term, ("sec", "dp", "seq"))
    grad_w_out = lax.dynamic_slice_in_dim(grad_total, lax.axis_index("seq") * rows_dev, rows_dev, 0)
    return (rewards, grad_w_out, grad_hidden)


def solution(mesh):
    placed = (
        P(("sec", "dp", "seq"), None, None),
        P(("sec", "dp", "seq"), None),
        P(("sec", "dp", "seq"), None),
        P(("sec", "dp", "seq"), None, None),
        P(("sec", "dp", "seq")),
        P(),
        P(),
        P(),
        P(None, None, "seq"),
        P("seq", None),
        P("seq", None),
        P(),
        P(("sec", "dp")),
        P(("sec", "dp")),
    )
    return jax.shard_map(
        local,
        mesh=mesh,
        in_specs=placed,
        out_specs=(P(("sec", "dp")), P("seq", None), P(("sec", "dp", "seq"), None, None)),
        check_vma=False,
    )
```

profile of v0, /device:TPU:2, one launch (start us, length us, event | category | flops | bytes accessed | tf_op | source)
XLA Modules:
  0.0 640.3 jit_solution(5430359469314224564)
XLA Ops:
  7.2 0.9 compare_and_fusion
  8.2 0.9 copy-done
  9.1 5.1 gather_fusion
  14.2 2.3 select_reduce_fusion
  17.3 1.3 convert_reduce_fusion
  18.5 1.4 fusion.22
  20.0 0.6 fusion.77
  20.7 1.8 fusion.24
  22.5 0.8 slice_reduce_fusion.1
  23.3 0.3 reduce_window_sum.30
  23.6 0.3 copy-done.31
  23.8 0.5 copy-done.33
  24.5 0.2 fusion.76
  24.7 0.2 multiply_add_fusion
  25.1 0.6 subtract_reduce_fusion.1
  26.0 1.7 multiply_reduce_fusion.3
  27.8 0.9 copy-done.4
  28.7 0.9 fusion.74
  29.8 0.5 neg.19
  30.3 88.0 %all-reduce.3.cloned.1.call-done = f32[32,512]{1,0:T(8,128)} async-done(((f32[32,512]{1,0:T(8,128)}), f32[32,512]{1,0:T(8,128)}) %all-reduce.3.cloned.1.call-update) | async-done | bytes 65552 | tf_op jit(solution)/shard_map/psum | solution.py:100
  118.3 1.0 multiply_reduce_fusion.8
  119.3 0.5 add_sqrt_fusion.2
  119.8 55.7 %all-gather.3.cloned.1.call-done = bf16[2048,2048]{1,0:T(8,128)(2,1)} async-done(((bf16[128,2048]{1,0:T(8,128)(2,1)}), bf16[2048,2048]{1,0:T(8,128)(2,1)}) %all-gather.3.cloned.1.call-update) | async-done | bytes 8388624 | tf_op jit(solution)/shard_map/all_gather | solution.py:115
  175.5 6.4 convolution_bitcast_fusion.1
  181.9 0.2 fusion.31
  182.1 1.6 fusion.32
  183.7 0.2 copy-done.1
  183.9 2.7 convert_reduce_fusion.1
  186.6 2.1 fusion.37
  188.8 47.4 %psum.21 = f32[16,512]{1,0:T(8,128)} all-reduce(f32[16,512]{1,0:T(8,128)S(1)} %fusion.59), channel_id=1, replica_groups=mesh['sec'=2,'dp'=8,'seq'=16] {'seq'}, use_global_device_ids=true, to_apply=%region_10.11 | all-reduce | flops 8192 | bytes 65536 | tf_op jit(solution)/shard_map/psum | solution.py:139
  236.2 1.2 multiply_reduce_fusion.9
  237.5 1.0 fusion.45
  238.4 0.4 multiply_convert_fusion
  238.8 1.7 fusion.35
  240.6 0.4 multiply_reduce_fusion.2
  241.0 0.6 convolution_bitcast_fusion.2
  241.5 1.0 copy-done.2
  242.5 0.2 copy-done.12
  242.7 0.8 multiply_reduce_fusion.1
  243.4 0.6 divide_convert_fusion.1
  244.0 0.8 copy-done.9
  244.8 8.1 %convolution_bitcast_fusion = f32[16,128,2048]{2,1,0:T(8,128)} fusion(bf16[16,128,1,128]{1,3,0,2:T(8,128)(2,1)S(1)} %multiply_convert_fusion, bf16[16,128,1,128]{1,3,0,2:T(8,128)(2,1)S(1)} %get-tuple-element.60, bf16[16,128,1,128]{1,3,0,2:T(8,128)(2,1)S(1)} %get-tuple-element.59, bf16[3,2048,128]{2,1,0:T(8,128)(2,1)S(1)} %copy-done.9), kind=kOutput, calls=%fused_computation.2 | convolution fusion | flops 3222798336 | bytes 19922944 | tf_op jit(solution)/shard_map/cfjk,jdk->cfd/dot_general | solution.py:182
  253.0 0.2 all-reduce.5.cloned.1.call-start
  253.2 100.2 %reduce-scatter.2.cloned.1.call-done = f32[1,128,2048]{2,1,0:T(8,128)} async-done(((f32[16,128,2048]{2,1,0:T(8,128)}), f32[1,128,2048]{2,1,0:T(8,128)}) %reduce-scatter.2.cloned.1.call-update) | async-done | bytes 1048592 | tf_op jit(solution)/shard_map/reduce_scatter | solution.py:181
  353.5 1.9 fusion.30
  355.5 0.2 copy-done.7
  355.7 2.1 multiply_reduce_fusion.7
  357.8 0.3 reduce_window_sum.37
  358.1 0.3 reduce_window_sum.38
  358.4 2.0 fusion.66
  360.8 2.7 fusion.27
  363.6 1.3 fusion.40
  364.9 1.0 scatter-add.10
  365.9 0.3 slice_add_fusion.1
  366.2 0.4 scatter-add.11
  366.6 0.3 slice_add_fusion
  366.8 0.4 scatter-add.14
  367.2 3.3 fusion.53
  370.5 0.7 copy-done.15
  371.2 3.2 fusion.18
  374.3 1.5 reduce_sum.224
  375.8 2.8 fusion.21
  378.7 253.5 %all-reduce.5.cloned.1.call-done = f32[2560,256]{1,0:T(8,128)} async-done(((f32[2560,256]{1,0:T(8,128)}), f32[2560,256]{1,0:T(8,128)}) %all-reduce.5.cloned.1.call-update) | async-done | bytes 2621456 | tf_op jit(solution)/shard_map/psum | solution.py:201
  632.2 1.6 constant_dynamic-slice_fusion
  (94 shorter events, 1.6 us)
Async XLA Ops:
  7.2 1.9 copy-start
  7.2 111.1 %all-reduce.3.cloned.1.call-start = ((), (), s32[]{:S(2)}) async-start(), calls=%async_computation.1 | async-start | bytes 131072 | tf_op jit(solution)/shard_map/psum | solution.py:100
  14.1 5.8 copy-start.20
  14.1 6.4 %copy-start.21 = (bf16[1,2560]{1,0:T(2,128)(2,1)S(1)}, bf16[1,2560]{1,0:T(2,128)(2,1)}, u32[]{:S(2)}) copy-start(bf16[1,2560]{1,0:T(2,128)(2,1)} %param.21) | copy-start | bytes 15364
  14.1 6.4 %copy-start.22 = (bf16[1,2560]{1,0:T(2,128)(2,1)S(1)}, bf16[1,2560]{1,0:T(2,128)(2,1)}, u32[]{:S(2)}) copy-start(bf16[1,2560]{1,0:T(2,128)(2,1)} %param.22) | copy-start | bytes 15364
  14.2 6.5 %copy-start.36 = (bf16[1,128,256]{2,1,0:T(8,128)(2,1)S(1)}, bf16[1,128,256]{2,1,0:T(8,128)(2,1)}, u32[]{:S(2)}) copy-start(bf16[1,128,256]{2,1,0:T(8,128)(2,1)} %param.23) | copy-start | bytes 196612
  16.5 159.0 %all-gather.3.cloned.1.call-start = ((), (), s32[]{:S(2)}) async-start(), calls=%async_computation.4 | async-start | bytes 8912896 | tf_op jit(solution)/shard_map/all_gather | solution.py:115
  16.5 4.1 copy-start.3
  18.5 3.9 copy-start.23
  20.0 2.5 copy-start.27
  20.7 1.8 copy-start.14
  20.7 1.8 copy-start.17
  23.3 0.6 copy-start.31
  23.8 0.5 copy-start.33
  24.9 2.8 copy-start.10
  27.7 1.0 copy-start.4
  27.8 2.0 copy-start.37
  27.8 1.0 copy-start.25
  29.7 323.8 %reduce-scatter.2.cloned.1.call-start = ((), (), s32[]{:S(2)}) async-start(), calls=%async_computation.2 | async-start | bytes 17825792 | tf_op jit(solution)/shard_map/reduce_scatter | solution.py:181
  181.9 2.0 copy-start.1
  183.9 4.8 copy-start.13
  183.9 52.3 %copy-start.16 = (f32[32,512]{1,0:T(8,128)S(1)}, f32[32,512]{1,0:T(8,128)}, u32[]{:S(2)}) copy-start(f32[32,512]{1,0:T(8,128)} %all-reduce.3.cloned.1.call-done) | copy-start | bytes 196612
  236.2 4.4 copy-start.6
  237.4 3.5 copy-start.35
  238.4 2.5 copy-start.8
  240.6 1.9 copy-start.2
  241.0 1.7 copy-start.12
  243.4 1.4 copy-start.9
  253.0 100.5 %copy-start.26 = (f32[128]{0:T(128)S(1)}, f32[128]{0:T(128)}, u32[]{:S(2)}) copy-start(f32[128]{0:T(128)} %copy-done.25) | copy-start | bytes 1540
  253.0 102.5 %copy-start.19 = (f32[1,2048]{1,0:T(1,128)S(1)}, f32[1,2048]{1,0:T(1,128)}, u32[]{:S(2)}) copy-start(f32[1,2048]{1,0:T(1,128)} %get-tuple-element.67) | copy-start | bytes 24580
  253.0 102.5 %copy-start.18 = (f32[1,2048]{1,0:T(1,128)S(1)}, f32[1,2048]{1,0:T(1,128)}, u32[]{:S(2)}) copy-start(f32[1,2048]{1,0:T(1,128)} %get-tuple-element.66) | copy-start | bytes 24580
  253.0 379.2 %all-reduce.5.cloned.1.call-start = ((), (), s32[]{:S(2)}) async-start(), calls=%async_computation.3 | async-start | bytes 5242880 | tf_op jit(solution)/shard_map/psum | solution.py:201
  353.5 2.0 copy-start.5
  353.5 2.2 copy-start.7
  355.6 2.7 copy-start.29
  355.6 2.7 copy-start.30
  355.6 2.7 copy-start.32
  355.6 2.7 copy-start.34
  355.6 5.0 copy-start.11
  370.5 0.7 copy-start.15
  370.5 0.7 copy-start.24
  370.5 0.7 copy-start.28
Sparse Core Ops, SparseCore 0:
  16.6 101.6 all-reduce.2
  120.9 54.6 all-gather.2
  253.1 100.3 reduce-scatter.1
  370.6 261.4 all-reduce.4
where the time goes:
time: 641 us; the launch traced here: 640 us
  waiting for transfers between devices  498 us (78%)
  blocking collectives  47.4 us (7%)
  matrix products  37.3 us (6%)
  other arithmetic  26.9 us (4%)
  local copies, waits for them, and re-layouts  15.9 us (2%)
  between operations  14.9 us (2%)
    psum x1, waiting for transfers between devices, local(): grad_total = lax.psum(grad_term, ('sec', 'dp', 'seq'))  253 us
    reduce_scatter x1, waiting for transfers between devices, local(): lax.psum_scatter(jnp.einsum('cfjk,jdk->cfd', d_proj, w_qkv, preferred_ele...  100 us
    psum x1, waiting for transfers between devices, local(): text_raw = lax.psum(text_part, 'seq')  88 us
    all_gather x1, waiting for transfers between devices, local(): lax.all_gather(normed_e.astype(jnp.bfloat16), 'seq', axis=0, tiled=True)  55.7 us
    psum x1, blocking collectives, local(): motion_emb = lax.psum(motion_part, 'seq')  47.4 us
  transfers between devices with their start and end apart: 4, of which 4 were waited for; matrix products, arithmetic and copies ran while one was open for 3% of the time, Pallas kernels for 0%

commit v1 on v0

--- a/solution.py
+++ b/solution.py
@@ -110,9 +110,48 @@
     x_clean = noisy.astype(jnp.float32) - level * eps_pred
     theta, path_east, path_north = local_path(x_clean)
     normed_e, scale_rms = embed(x_clean, path_east, path_north, w_embed, root_rows)
+
+    def hold_field_on_mesh(block_in, which_dim):
+        along_axis = "seq"
+        reached, latest, lower = (
+            jax.lax.axis_size(along_axis),
+            jax.lax.axis_index(along_axis),
+            block_in.shape[which_dim],
+        )
+        history = []
+        for dev, dev_j in enumerate(block_in.shape):
+            history.append(dev_j * reached if dev == which_dim else dev_j)
+        after = lax.dynamic_update_slice_in_dim(
+            jnp.zeros(history, block_in.dtype), block_in, latest * lower, axis=which_dim
+        )
+        t1 = opened = block_in
+        c = 1
+        while c < reached // 2 + 1:
+            copies = []
+            dev = 0
+            while dev < reached:
+                copies.append((dev, (dev + 1) % reached))
+                dev += 1
+            t1 = jax.lax.ppermute(t1, axis_name=along_axis, perm=copies)
+            after = lax.dynamic_update_slice_in_dim(
+                after, t1, (latest - c) % reached * lower, axis=which_dim
+            )
+            if 2 * c < reached:
+                block_list = []
+                dev = 0
+                while dev < reached:
+                    block_list.append((dev, (dev - 1) % reached))
+                    dev += 1
+                opened = jax.lax.ppermute(opened, axis_name=along_axis, perm=block_list)
+                after = lax.dynamic_update_slice_in_dim(
+                    after, opened, (latest + c) % reached * lower, axis=which_dim
+                )
+            c += 1
+        return after
+
     projected = jnp.einsum(
         "cfd,jdk->cfjk",
-        lax.all_gather(normed_e.astype(jnp.bfloat16), "seq", axis=0, tiled=True),
+        hold_field_on_mesh(normed_e.astype(jnp.bfloat16), 0),
         w_qkv,
         preferred_element_type=jnp.float32,
     )

time: 641 us -> 670 us (1.045)
  starting transfers between devices: 0.34 us -> 23.5 us
  local copies, waits for them, and re-layouts: 15.9 us -> 36.4 us
  waiting for transfers between devices: 498 us -> 482 us
    all_gather x1 -> x0, waiting for transfers between devices: 55.7 us -> none  [local(): lax.all_gather(normed_e.astype(jnp.bfloat16), 'seq', axis=0, tiled=True)]
    ppermute x0 -> x15, waiting for transfers between devices: none -> 32.7 us  [the longest x8 27.9 us: hold_field_on_mesh(): t1 = jax.lax.ppermute(t1, axis_name=along_axis, perm=copies)]
    ppermute x0 -> x15, starting transfers between devices: none -> 23.4 us  [the longest x7 22.9 us: hold_field_on_mesh(): opened = jax.lax.ppermute(opened, axis_name=along_axis, perm=block_list)]
    dynamic_update_slice x0 -> x15, local copies, waits for them, and re-layouts: none -> 18.9 us  [the longest x8 9.89 us: hold_field_on_mesh(): lax.dynamic_update_slice_in_dim(after, t1, (latest - c) % reached * lower...]
    psum x1, waiting for transfers between devices: 88 us -> 96 us  [local(): text_raw = lax.psum(text_part, 'seq')]
  transfers between devices with their start and end apart: 4 -> 18, of which waited for: 4 -> 13; matrix products, arithmetic and copies ran while one was open for 3% -> 5% of each run, Pallas kernels for 0% -> 0%
where the time goes in v1:
time: 670 us; the launch traced here: 668 us
  waiting for transfers between devices  482 us (72%)
  blocking collectives  46.5 us (7%)
  matrix products  38.1 us (6%)
  local copies, waits for them, and re-layouts  36.4 us (5%)
  other arithmetic  26.8 us (4%)
  starting transfers between devices  23.5 us (4%)
  between operations  15.2 us (2%)
    psum x1, waiting for transfers between devices, local(): grad_total = lax.psum(grad_term, ('sec', 'dp', 'seq'))  254 us
    reduce_scatter x1, waiting for transfers between devices, local(): lax.psum_scatter(jnp.einsum('cfjk,jdk->cfd', d_proj, w_qkv, preferred_ele...  99.1 us
    psum x1, waiting for transfers between devices, local(): text_raw = lax.psum(text_part, 'seq')  96 us
    psum x1, blocking collectives, local(): motion_emb = lax.psum(motion_part, 'seq')  46.5 us
    ppermute x8, waiting for transfers between devices, hold_field_on_mesh(): t1 = jax.lax.ppermute(t1, axis_name=along_axis, perm=copies)  27.9 us
    ppermute x7, starting transfers between devices, hold_field_on_mesh(): opened = jax.lax.ppermute(opened, axis_name=along_axis, perm=block_list)  22.9 us
  transfers between devices with their start and end apart: 18, of which 13 were waited for; matrix products, arithmetic and copies ran while one was open for 5% of the time, Pallas kernels for 0%

profile of v1, /device:TPU:2, one launch (start us, length us, event | category | flops | bytes accessed | tf_op | source)
XLA Modules:
  0.0 668.5 jit_solution(13290236403225343962)
XLA Ops:
  7.2 1.4 convert_reduce_fusion
  8.7 1.4 fusion.27
  12.1 1.9 fusion.29
  18.4 2.6 multiply_reduce_fusion.3
  21.0 1.1 broadcast_in_dim.26
  22.3 1.0 constant_dynamic-update-slice_fusion.15
  23.2 3.2 copy-done.5
  26.4 5.3 collective-permute-start.1
  31.7 7.2 %collective-permute-done = bf16[1,128,2048]{2,1,0:T(8,128)(2,1)} collective-permute-done((bf16[1,128,2048]{2,1,0:T(8,128)(2,1)}, bf16[1,128,2048]{2,1,0:T(8,128)(2,1)}, u32[]{:S(2)}, u32[]{:S(2)}) %collective-permute-start) | collective-permute-done | bytes 524320 | tf_op jit(solution)/shard_map/ppermute | solution.py:135
  38.9 3.0 collective-permute-start.3
  42.0 7.1 %collective-permute-done.2 = bf16[1,128,2048]{2,1,0:T(8,128)(2,1)} collective-permute-done((bf16[1,128,2048]{2,1,0:T(8,128)(2,1)}, bf16[1,128,2048]{2,1,0:T(8,128)(2,1)}, u32[]{:S(2)}, u32[]{:S(2)}) %collective-permute-start.2) | collective-permute-done | bytes 524320 | tf_op jit(solution)/shard_map/ppermute | solution.py:135
  49.1 5.1 gather_fusion
  54.1 2.2 select_reduce_fusion
  57.2 2.9 collective-permute-start.5
  60.2 96.0 %all-reduce.3.cloned.1.call-done = f32[32,512]{1,0:T(8,128)} async-done(((f32[32,512]{1,0:T(8,128)}), f32[32,512]{1,0:T(8,128)}) %all-reduce.3.cloned.1.call-update) | async-done | bytes 65552 | tf_op jit(solution)/shard_map/psum | solution.py:100
  156.2 1.0 multiply_reduce_fusion.8
  158.1 1.9 constant_dynamic-update-slice_fusion.14
  160.0 2.5 collective-permute-start.7
  162.6 1.9 constant_dynamic-update-slice_fusion.13
  164.5 2.8 collective-permute-done.6
  167.2 1.9 constant_dynamic-update-slice_fusion.12
  169.1 1.9 constant_dynamic-update-slice_fusion.11
  171.0 3.0 collective-permute-start.9
  174.0 1.9 constant_dynamic-update-slice_fusion.10
  175.9 1.1 collective-permute-done.8
  177.1 1.9 constant_dynamic-update-slice_fusion.9
  178.9 0.8 constant_dynamic-update-slice_fusion.8
  179.8 0.9 collective-permute-done.9
  180.7 3.1 collective-permute-start.11
  183.8 0.8 constant_dynamic-update-slice_fusion.7
  184.6 2.2 collective-permute-done.10
  186.9 0.8 constant_dynamic-update-slice_fusion.6
  187.7 0.8 constant_dynamic-update-slice_fusion.5
  188.6 1.9 collective-permute-done.11
  190.5 3.1 collective-permute-start.13
  193.6 0.8 constant_dynamic-update-slice_fusion.4
  194.5 2.2 collective-permute-done.12
  197.5 0.9 constant_dynamic-update-slice_fusion.2
  198.4 2.0 collective-permute-done.13
  200.3 0.8 constant_dynamic-update-slice_fusion.1
  201.2 5.3 collective-permute-done.14
  206.5 0.8 constant_dynamic-update-slice_fusion
  207.3 5.9 fusion.4
  213.5 1.6 fusion.37
  215.3 2.7 convert_reduce_fusion.1
  217.9 2.1 fusion.42
  220.2 46.5 %psum.21 = f32[16,512]{1,0:T(8,128)} all-reduce(f32[16,512]{1,0:T(8,128)S(1)} %fusion.64), channel_id=1, replica_groups=mesh['sec'=2,'dp'=8,'seq'=16] {'seq'}, use_global_device_ids=true, to_apply=%region_10.11 | all-reduce | flops 8192 | bytes 65536 | tf_op jit(solution)/shard_map/psum | solution.py:178
  266.7 1.2 multiply_reduce_fusion.9
  268.0 1.0 fusion.50
  269.4 1.9 fusion.40
  274.4 8.1 %convolution_bitcast_fusion = f32[16,128,2048]{2,1,0:T(8,128)} fusion(bf16[16,128,1,128]{1,3,0,2:T(8,128)(2,1)S(1)} %multiply_convert_fusion, bf16[16,128,1,128]{1,3,0,2:T(8,128)(2,1)S(1)} %get-tuple-element.62, bf16[16,128,1,128]{1,3,0,2:T(8,128)(2,1)S(1)} %get-tuple-element.61, bf16[3,2048,128]{2,1,0:T(8,128)(2,1)S(1)} %copy-done.10), kind=kOutput, calls=%fused_computation.4 | convolution fusion | flops 3222798336 | bytes 19922944 | tf_op jit(solution)/shard_map/cfjk,jdk->cfd/dot_general | solution.py:221
  282.7 99.1 %reduce-scatter.2.cloned.1.call-done = f32[1,128,2048]{2,1,0:T(8,128)} async-done(((f32[16,128,2048]{2,1,0:T(8,128)}), f32[1,128,2048]{2,1,0:T(8,128)}) %reduce-scatter.2.cloned.1.call-update) | async-done | bytes 1048592 | tf_op jit(solution)/shard_map/reduce_scatter | solution.py:220
  381.8 1.9 fusion.35
  383.9 2.1 multiply_reduce_fusion.7
  386.7 2.0 fusion.71
  389.1 2.7 fusion.32
  391.8 1.3 fusion.45
  393.2 1.0 scatter-add.10
  395.5 3.3 fusion.58
  398.8 3.2 fusion.23
  402.0 1.5 reduce_sum.224
  403.4 2.8 fusion.26
  406.3 254.1 %all-reduce.5.cloned.1.call-done = f32[2560,256]{1,0:T(8,128)} async-done(((f32[2560,256]{1,0:T(8,128)}), f32[2560,256]{1,0:T(8,128)}) %all-reduce.5.cloned.1.call-update) | async-done | bytes 2621456 | tf_op jit(solution)/shard_map/psum | solution.py:240
  660.4 1.6 constant_dynamic-slice_fusion
  (137 shorter events, 15.0 us)
Async XLA Ops:
  7.2 41.9 %copy-start = (bf16[3088,512]{1,0:T(8,128)(2,1)S(1)}, bf16[3088,512]{1,0:T(8,128)(2,1)}, u32[]{:S(2)}) copy-start(bf16[3088,512]{1,0:T(8,128)(2,1)} %param.30) | copy-start | bytes 9486340
  7.2 149.1 %all-reduce.3.cloned.1.call-start = ((), (), s32[]{:S(2)}) async-start(), calls=%async_computation.1 | async-start | bytes 131072 | tf_op jit(solution)/shard_map/psum | solution.py:100
  8.6 6.2 copy-start.24
  10.1 4.8 copy-start.28
  11.5 0.6 copy-start.15
  11.5 2.5 copy-start.18
  14.8 0.6 copy-start.32
  15.4 0.5 copy-start.34
  16.5 5.6 copy-start.11
  18.4 3.7 copy-start.19
  18.4 3.7 copy-start.21
  21.0 1.1 copy-start.26
  21.0 1.2 copy-start.3
  21.0 20.8 %copy-start.23 = (s32[32,32]{1,0:T(8,128)S(1)}, s32[32,32]{1,0:T(8,128)}, u32[]{:S(2)}) copy-start(s32[32,32]{1,0:T(8,128)} %param.31) | copy-start | bytes 12292
  23.2 3.2 copy-start.5
  26.4 12.5 %collective-permute-start = (bf16[1,128,2048]{2,1,0:T(8,128)(2,1)}, bf16[1,128,2048]{2,1,0:T(8,128)(2,1)}, u32[]{:S(2)}, u32[]{:S(2)}) collective-permute-start(bf16[1,128,2048]{2,1,0:T(8,128)(2,1)} %get-tuple-element.58), channel_id=1, source_target_pairs={{0,1},{1,2},{2,3},{3,4},{4,5},{5,6},{6,7},{7,8},{8,9},{9,10},{10,1... | collective-permute-start | bytes 1572872 | tf_op jit(solution)/shard_map/ppermute | solution.py:135
  26.4 12.5 %collective-permute-start.1 = (bf16[1,128,2048]{2,1,0:T(8,128)(2,1)}, bf16[1,128,2048]{2,1,0:T(8,128)(2,1)}, u32[]{:S(2)}, u32[]{:S(2)}) collective-permute-start(bf16[1,128,2048]{2,1,0:T(8,128)(2,1)} %get-tuple-element.58), channel_id=1, source_target_pairs={{0,15},{1,0},{2,1},{3,2},{4,3},{5,4},{6,5},{7,6},{8,7},{9,8},{10,9... | collective-permute-start | bytes 1572872 | tf_op jit(solution)/shard_map/ppermute | solution.py:145
  38.9 10.1 %collective-permute-start.2 = (bf16[1,128,2048]{2,1,0:T(8,128)(2,1)}, bf16[1,128,2048]{2,1,0:T(8,128)(2,1)}, u32[]{:S(2)}, u32[]{:S(2)}) collective-permute-start(bf16[1,128,2048]{2,1,0:T(8,128)(2,1)} %collective-permute-done), channel_id=1, source_target_pairs={{0,1},{1,2},{2,3},{3,4},{4,5},{5,6},{6,7},{7,8},{8,9},{9,10},{10,1... | collective-permute-start | bytes 1572872 | tf_op jit(solution)/shard_map/ppermute | solution.py:135
  38.9 18.3 %collective-permute-start.3 = (bf16[1,128,2048]{2,1,0:T(8,128)(2,1)}, bf16[1,128,2048]{2,1,0:T(8,128)(2,1)}, u32[]{:S(2)}, u32[]{:S(2)}) collective-permute-start(bf16[1,128,2048]{2,1,0:T(8,128)(2,1)} %collective-permute-done.1), channel_id=1, source_target_pairs={{0,15},{1,0},{2,1},{3,2},{4,3},{5,4},{6,5},{7,6},{8,7},{9,8},{10,9... | collective-permute-start | bytes 1572872 | tf_op jit(solution)/shard_map/ppermute | solution.py:145
  49.0 108.1 %collective-permute-start.4 = (bf16[1,128,2048]{2,1,0:T(8,128)(2,1)}, bf16[1,128,2048]{2,1,0:T(8,128)(2,1)}, u32[]{:S(2)}, u32[]{:S(2)}) collective-permute-start(bf16[1,128,2048]{2,1,0:T(8,128)(2,1)} %collective-permute-done.2), channel_id=1, source_target_pairs={{0,1},{1,2},{2,3},{3,4},{4,5},{5,6},{6,7},{7,8},{8,9},{9,10},{10,1... | collective-permute-start | bytes 1572872 | tf_op jit(solution)/shard_map/ppermute | solution.py:135
  49.1 7.6 %copy-start.37 = (f32[16]{0:T(128)S(1)}, f32[16]{0:T(128)}, u32[]{:S(2)}) copy-start(f32[16]{0:T(128)} %param.33) | copy-start | bytes 196
  56.4 325.3 %reduce-scatter.2.cloned.1.call-start = ((), (), s32[]{:S(2)}) async-start(), calls=%async_computation.2 | async-start | bytes 17825792 | tf_op jit(solution)/shard_map/reduce_scatter | solution.py:220
  57.2 102.8 %collective-permute-start.5 = (bf16[1,128,2048]{2,1,0:T(8,128)(2,1)}, bf16[1,128,2048]{2,1,0:T(8,128)(2,1)}, u32[]{:S(2)}, u32[]{:S(2)}) collective-permute-start(bf16[1,128,2048]{2,1,0:T(8,128)(2,1)} %collective-permute-done.3), channel_id=1, source_target_pairs={{0,15},{1,0},{2,1},{3,2},{4,3},{5,4},{6,5},{7,6},{8,7},{9,8},{10,9... | collective-permute-start | bytes 1572872 | tf_op jit(solution)/shard_map/ppermute | solution.py:145
  157.2 10.0 %collective-permute-start.6 = (bf16[1,128,2048]{2,1,0:T(8,128)(2,1)}, bf16[1,128,2048]{2,1,0:T(8,128)(2,1)S(1)}, u32[]{:S(2)}, u32[]{:S(2)}) collective-permute-start(bf16[1,128,2048]{2,1,0:T(8,128)(2,1)} %collective-permute-done.4), channel_id=1, source_target_pairs={{0,1},{1,2},{2,3},{3,4},{4,5},{5,6},{6,7},{7,8},{8,9},{9,10},{10,1... | collective-permute-start | bytes 1572872 | tf_op jit(solution)/shard_map/ppermute | solution.py:135
  160.0 11.0 %collective-permute-start.7 = (bf16[1,128,2048]{2,1,0:T(8,128)(2,1)}, bf16[1,128,2048]{2,1,0:T(8,128)(2,1)S(1)}, u32[]{:S(2)}, u32[]{:S(2)}) collective-permute-start(bf16[1,128,2048]{2,1,0:T(8,128)(2,1)} %collective-permute-done.5), channel_id=1, source_target_pairs={{0,15},{1,0},{2,1},{3,2},{4,3},{5,4},{6,5},{7,6},{8,7},{9,8},{10,9... | collective-permute-start | bytes 1572872 | tf_op jit(solution)/shard_map/ppermute | solution.py:145
  167.2 9.8 %collective-permute-start.8 = (bf16[1,128,2048]{2,1,0:T(8,128)(2,1)S(1)}, bf16[1,128,2048]{2,1,0:T(8,128)(2,1)S(1)}, u32[]{:S(2)}, u32[]{:S(2)}) collective-permute-start(bf16[1,128,2048]{2,1,0:T(8,128)(2,1)S(1)} %collective-permute-done.6), channel_id=1, source_target_pairs={{0,1},{1,2},{2,3},{3,4},{4,5},{5,6},{6,7},{7,8},{8,9},{9,10},{10,1... | collective-permute-start | bytes 1572872 | tf_op jit(solution)/shard_map/ppermute | solution.py:135
  171.0 9.7 %collective-permute-start.9 = (bf16[1,128,2048]{2,1,0:T(8,128)(2,1)S(1)}, bf16[1,128,2048]{2,1,0:T(8,128)(2,1)S(1)}, u32[]{:S(2)}, u32[]{:S(2)}) collective-permute-start(bf16[1,128,2048]{2,1,0:T(8,128)(2,1)S(1)} %collective-permute-done.7), channel_id=1, source_target_pairs={{0,15},{1,0},{2,1},{3,2},{4,3},{5,4},{6,5},{7,6},{8,7},{9,8},{10,9... | collective-permute-start | bytes 1572872 | tf_op jit(solution)/shard_map/ppermute | solution.py:145
  177.0 9.8 %collective-permute-start.10 = (bf16[1,128,2048]{2,1,0:T(8,128)(2,1)S(1)}, bf16[1,128,2048]{2,1,0:T(8,128)(2,1)S(1)}, u32[]{:S(2)}, u32[]{:S(2)}) collective-permute-start(bf16[1,128,2048]{2,1,0:T(8,128)(2,1)S(1)} %collective-permute-done.8), channel_id=1, source_target_pairs={{0,1},{1,2},{2,3},{3,4},{4,5},{5,6},{6,7},{7,8},{8,9},{9,10},{10,1... | collective-permute-start | bytes 1572872 | tf_op jit(solution)/shard_map/ppermute | solution.py:135
  180.7 9.8 %collective-permute-start.11 = (bf16[1,128,2048]{2,1,0:T(8,128)(2,1)S(1)}, bf16[1,128,2048]{2,1,0:T(8,128)(2,1)S(1)}, u32[]{:S(2)}, u32[]{:S(2)}) collective-permute-start(bf16[1,128,2048]{2,1,0:T(8,128)(2,1)S(1)} %collective-permute-done.9), channel_id=1, source_target_pairs={{0,15},{1,0},{2,1},{3,2},{4,3},{5,4},{6,5},{7,6},{8,7},{9,8},{10,9... | collective-permute-start | bytes 1572872 | tf_op jit(solution)/shard_map/ppermute | solution.py:145
  186.9 9.8 %collective-permute-start.12 = (bf16[1,128,2048]{2,1,0:T(8,128)(2,1)S(1)}, bf16[1,128,2048]{2,1,0:T(8,128)(2,1)S(1)}, u32[]{:S(2)}, u32[]{:S(2)}) collective-permute-start(bf16[1,128,2048]{2,1,0:T(8,128)(2,1)S(1)} %collective-permute-done.10), channel_id=1, source_target_pairs={{0,1},{1,2},{2,3},{3,4},{4,5},{5,6},{6,7},{7,8},{8,9},{9,10},{10,1... | collective-permute-start | bytes 1572872 | tf_op jit(solution)/shard_map/ppermute | solution.py:135
  188.6 18.8 %copy-start.9 = (bf16[3,2048,128]{2,1,0:T(8,128)(2,1)S(1)}, bf16[3,2048,128]{2,1,0:T(8,128)(2,1)}, u32[]{:S(2)}) copy-start(bf16[3,2048,128]{2,1,0:T(8,128)(2,1)} %param.28) | copy-start | bytes 4718596
  190.5 9.8 %collective-permute-start.13 = (bf16[1,128,2048]{2,1,0:T(8,128)(2,1)S(1)}, bf16[1,128,2048]{2,1,0:T(8,128)(2,1)S(1)}, u32[]{:S(2)}, u32[]{:S(2)}) collective-permute-start(bf16[1,128,2048]{2,1,0:T(8,128)(2,1)S(1)} %collective-permute-done.11), channel_id=1, source_target_pairs={{0,15},{1,0},{2,1},{3,2},{4,3},{5,4},{6,5},{7,6},{8,7},{9,8},{10,9... | collective-permute-start | bytes 1572872 | tf_op jit(solution)/shard_map/ppermute | solution.py:145
  196.7 9.8 %collective-permute-start.14 = (bf16[1,128,2048]{2,1,0:T(8,128)(2,1)S(1)}, bf16[1,128,2048]{2,1,0:T(8,128)(2,1)S(1)}, u32[]{:S(2)}, u32[]{:S(2)}) collective-permute-start(bf16[1,128,2048]{2,1,0:T(8,128)(2,1)S(1)} %collective-permute-done.12), channel_id=1, source_target_pairs={{0,1},{1,2},{2,3},{3,4},{4,5},{5,6},{6,7},{7,8},{8,9},{9,10},{10,1... | collective-permute-start | bytes 1572872 | tf_op jit(solution)/shard_map/ppermute | solution.py:135
  213.3 2.0 copy-start.1
  215.3 4.8 copy-start.14
  215.3 51.4 %copy-start.17 = (f32[32,512]{1,0:T(8,128)S(1)}, f32[32,512]{1,0:T(8,128)}, u32[]{:S(2)}) copy-start(f32[32,512]{1,0:T(8,128)} %all-reduce.3.cloned.1.call-done) | copy-start | bytes 196612
  266.7 4.6 copy-start.6
  266.7 4.9 copy-start.8
  268.0 4.2 copy-start.36
  269.0 3.3 copy-start.2
  269.0 3.3 copy-start.13
  273.0 1.4 copy-start.10
  282.6 99.2 %copy-start.27 = (f32[128]{0:T(128)S(1)}, f32[128]{0:T(128)}, u32[]{:S(2)}) copy-start(f32[128]{0:T(128)} %copy-done.26) | copy-start | bytes 1540
  282.6 101.2 %copy-start.20 = (f32[1,2048]{1,0:T(1,128)S(1)}, f32[1,2048]{1,0:T(1,128)}, u32[]{:S(2)}) copy-start(f32[1,2048]{1,0:T(1,128)} %copy-done.19) | copy-start | bytes 24580
  282.6 101.2 %copy-start.22 = (f32[1,2048]{1,0:T(1,128)S(1)}, f32[1,2048]{1,0:T(1,128)}, u32[]{:S(2)}) copy-start(f32[1,2048]{1,0:T(1,128)} %copy-done.21) | copy-start | bytes 24580
  282.6 377.8 %all-reduce.5.cloned.1.call-start = ((), (), s32[]{:S(2)}) async-start(), calls=%async_computation.3 | async-start | bytes 5242880 | tf_op jit(solution)/shard_map/psum | solution.py:240
  282.6 104.0 %copy-start.30 = (f32[128]{0:T(128)S(1)}, f32[128]{0:T(128)}, u32[]{:S(2)}) copy-start(f32[128]{0:T(128)} %get-tuple-element.49) | copy-start | bytes 1540
  282.6 104.0 %copy-start.31 = (f32[128]{0:T(128)S(1)}, f32[128]{0:T(128)}, u32[]{:S(2)}) copy-start(f32[128]{0:T(128)} %get-tuple-element.50) | copy-start | bytes 1540
  282.7 104.0 %copy-start.33 = (f32[128]{0:T(128)S(1)}, f32[128]{0:T(128)}, u32[]{:S(2)}) copy-start(f32[128]{0:T(128)} %copy-done.32) | copy-start | bytes 1540
  282.7 104.0 %copy-start.35 = (f32[1,128]{1,0:T(1,128)S(1)}, f32[1,128]{1,0:T(1,128)}, u32[]{:S(2)}) copy-start(f32[1,128]{1,0:T(1,128)} %copy-done.34) | copy-start | bytes 1540
  381.8 2.0 copy-start.4
  381.8 2.2 copy-start.7
  381.8 7.2 %copy-start.12 = (f32[1,128,1]{2,1,0:T(8,128)S(1)}, f32[1,128,1]{2,1,0:T(8,128)}, u32[]{:S(2)}) copy-start(f32[1,128,1]{2,1,0:T(8,128)} %copy-done.11) | copy-start | bytes 1540
  395.5 3.3 copy-start.16
  395.5 3.3 copy-start.25
  395.5 3.3 copy-start.29
Sparse Core Ops, SparseCore 0:
  56.5 99.6 all-reduce.2
  282.7 98.9 reduce-scatter.1
  398.9 261.4 all-reduce.4
